TPU v7x, 512 devices: a whole 4x8x8 slice. The times are simulated.
512 devices in a mesh: island: 16 (over z, x_hi), fsdp: 32 (over y, x_lo, core).
Axes of the slice: x: 4 (x_hi: 2, x_lo: 2; x = x_hi * 2 + x_lo), y: 8, z: 8, core: 2. Of those that a mesh axis runs over, the one named last changes fastest.
Arguments:
- block_input: bfloat16 [65536, 8192], P(('island', 'fsdp')), may hold values from -170 to 170
- lang_ids: int32 [65536], P(('island', 'fsdp')), may hold values from 0 to 15
- queries: bfloat16 [65536, 4096], P(('island', 'fsdp')), may hold values from -52 to 52
- saved_keys: bfloat16 [65536, 512], P(('island', 'fsdp')), may hold values from -4 to 4
- out_grad: bfloat16 [65536, 4096], P(('island', 'fsdp')), may hold values from -70 to 70
- local_wv: bfloat16 [16, 8192, 512], P('island', 'fsdp'), may hold values from -8 to 8
- local_gain: bfloat16 [16, 16, 8192], P('island'), may hold values from -3 to 5
- outer_wv: float32 [8192, 512], P('fsdp', 'island'), may hold values from -4 to 4
- wv_momentum: float32 [8192, 512], P('fsdp', 'island'), may hold values from -1.8 to 1.8
- outer_gain: float32 [16, 8192], P('island', 'fsdp'), may hold values from 0.5 to 1.5
- gain_momentum: float32 [16, 8192], P('island', 'fsdp'), may hold values from -1.8 to 1.8
Outputs:
- new_outer_wv: float32 [8192, 512], P('fsdp', 'island')
- new_wv_momentum: float32 [8192, 512], P('fsdp', 'island')
- new_outer_gain: float32 [16, 8192], P('island', 'fsdp')
- new_gain_momentum: float32 [16, 8192], P('island', 'fsdp')
All inputs are finite; a program needn't handle non-finite values.
Results may differ from a plain program's by a relative error of at most 0.00045.
Values may be sent and summed in bfloat16 or wider, within the bound.
No kernel may reach another device: no remote copies, remote signals or barrier semaphores. Data moves between devices by JAX's collectives and lax.ppermute only.
A program may use at most 64 MiB of HBM per device.

v0:
```python
import jax
import jax.numpy as jnp
from jax import lax
from jax.sharding import PartitionSpec as P

HEADS = 32
KV_HEADS = 4
HEAD_DIM = 128
EPSILON = 1e-05
MOMENTUM = 0.9
OUTER_RATE = 0.7
CLIP_SHARE = 0.25


def normalize(input_rows):
    widened = input_rows.astype(jnp.float32)
    average = jnp.mean(widened, axis=-1, keepdims=True)
    centered = widened - average
    variance = jnp.mean(centered * centered, axis=-1, keepdims=True)
    return centered * lax.rsqrt(variance + EPSILON)


def value_grad(query_rows, key_block, grad_rows):
    length = query_rows.shape[0]
    group = HEADS // KV_HEADS
    query_four = query_rows.reshape(length, KV_HEADS, group, HEAD_DIM)
    key_three = key_block.reshape(length, KV_HEADS, HEAD_DIM)
    scores = jnp.einsum(
        "tkgd,skd->kgts", query_four, key_three, preferred_element_type=jnp.float32
    ) * HEAD_DIM ** (-0.5)
    position = jnp.arange(length, dtype=jnp.int32)
    causal = position[:, None] >= position[None, :]
    scores = jnp.where(causal, scores, -jnp.inf)
    row_top = jnp.max(scores, axis=-1, keepdims=True)
    exponent = jnp.exp(scores - row_top)
    weights_bf = (exponent / jnp.sum(exponent, axis=-1, keepdims=True)).astype(jnp.bfloat16)
    grad_four = grad_rows.reshape(length, KV_HEADS, group, HEAD_DIM)
    values = jnp.einsum("kgts,tkgd->skd", weights_bf, grad_four, preferred_element_type=jnp.float32)
    return values.reshape(length, KV_HEADS * HEAD_DIM).astype(jnp.bfloat16)


def body(
    block_input,
    lang_ids,
    queries,
    saved_keys,
    out_grad,
    local_wv,
    local_gain,
    outer_wv,
    wv_momentum,
    outer_gain,
    gain_momentum,
):
    width = block_input.shape[1]
    fsdp_count = lax.axis_size("fsdp")
    island_count = lax.axis_size("island")
    col_block = width // fsdp_count
    kv_width = local_wv.shape[2]
    lang_count = local_gain.shape[1]
    weight_scale = width ** (-0.5)
    col_begin = lax.axis_index("fsdp") * col_block
    standard = normalize(block_input)
    lang_table = lang_ids[None, :] == jnp.arange(lang_count, dtype=jnp.int32)[:, None]
    gain_rows = jnp.dot(
        lang_table.astype(jnp.bfloat16).T, local_gain[0], preferred_element_type=jnp.float32
    )
    normed = (standard * gain_rows).astype(jnp.bfloat16)
    values_grad = value_grad(queries, saved_keys, out_grad)
    weight_rows = local_wv[0]
    col_normed = lax.all_to_all(normed, "fsdp", split_axis=1, concat_axis=0, tiled=True)
    input_grad = (
        jnp.dot(
            values_grad,
            lax.all_gather(weight_rows, "fsdp", axis=0, tiled=True).T,
            preferred_element_type=jnp.float32,
        )
        * weight_scale
    )
    gain_part = jnp.dot(
        lang_table.astype(jnp.float32), standard * input_grad, precision=lax.Precision.HIGHEST
    )
    gain_grad = lax.psum(gain_part, "fsdp")
    wv_grad = (
        jnp.dot(
            col_normed.T,
            lax.all_gather(values_grad, "fsdp", axis=0, tiled=True),
            preferred_element_type=jnp.float32,
        )
        * weight_scale
    )
    wv_square = jnp.sum(wv_grad * wv_grad)
    weight_square = lax.psum(wv_square, "fsdp")
    gain_square = jnp.sum(gain_grad * gain_grad)
    own_grad = lax.dynamic_slice_in_dim(gain_grad, col_begin, col_block, 1)
    wv_clip = jnp.minimum(1.0, CLIP_SHARE * (width * kv_width) ** 0.5 / jnp.sqrt(weight_square))
    gain_clip = jnp.minimum(1.0, CLIP_SHARE * (lang_count * width) ** 0.5 / jnp.sqrt(gain_square))
    new_wv = weight_rows.astype(jnp.float32) - wv_clip * wv_grad
    own_gain = lax.dynamic_slice_in_dim(local_gain[0], col_begin, col_block, 1).astype(jnp.float32)
    new_gain = own_gain - gain_clip * own_grad
    wv_share = kv_width // island_count
    gain_share = lang_count // island_count
    total_wv, total_gain = lax.psum((new_wv, new_gain), "island")
    island_at = lax.axis_index("island")
    total_wv = lax.dynamic_slice_in_dim(total_wv, island_at * wv_share, wv_share, 1)
    total_gain = lax.dynamic_slice_in_dim(total_gain, island_at * gain_share, gain_share, 0)
    delta_wv = outer_wv - total_wv / island_count
    momentum_wv = MOMENTUM * wv_momentum + delta_wv
    result_wv = outer_wv - OUTER_RATE * (delta_wv + MOMENTUM * momentum_wv)
    delta_gain = outer_gain - total_gain / island_count
    momentum_gain = MOMENTUM * gain_momentum + delta_gain
    result_gain = outer_gain - OUTER_RATE * (delta_gain + MOMENTUM * momentum_gain)
    return (result_wv, momentum_wv, result_gain, momentum_gain)


def solution(mesh):
    in_specs = (
        P(("island", "fsdp"), None),
        P(("island", "fsdp")),
        P(("island", "fsdp"), None),
        P(("island", "fsdp"), None),
        P(("island", "fsdp"), None),
        P("island", "fsdp", None),
        P("island", None, None),
        P("fsdp", "island"),
        P("fsdp", "island"),
        P("island", "fsdp"),
        P("island", "fsdp"),
    )
    out_specs = (P("fsdp", "island"), P("fsdp", "island"), P("island", "fsdp"), P("island", "fsdp"))
    return jax.shard_map(body, mesh=mesh, in_specs=in_specs, out_specs=out_specs, check_vma=False)
```

profile of v0, /device:TPU:32, one launch (start us, length us, event | category | flops | bytes accessed | tf_op | source)
XLA Modules:
  0.0 690.6 jit_solution(18145128111917954765)
XLA Ops:
  7.2 0.0 all-gather.4.cloned.1.call-start
  7.2 1.4 copy.48
  8.7 0.9 reshape.40
  9.6 1.6 copy.46
  11.3 2.3 fusion.33
  13.5 0.0 copy-start
  13.6 2.8 fusion.8
  16.4 0.0 copy-start.7
  16.4 0.0 copy-start.8
  16.4 0.0 all-gather.4.cloned.1.call-update
  16.4 0.0 all-gather.6.cloned.1.call-start
  16.5 0.7 all-gather.6.cloned.1.call-update
  17.2 0.0 copy-done
  17.2 0.4 convert_reduce_fusion
  17.5 0.7 fusion.6
  18.3 0.0 copy-done.7
  18.3 0.0 copy-done.8
  18.3 0.8 fusion.2
  19.1 0.0 copy-start.1
  19.1 1.6 copy.70
  20.7 9.9 %all-to-all-start = ((bf16[128,32,256]{2,0,1:T(8,128)(2,1)}), bf16[128,32,256]{2,0,1:T(8,128)(2,1)}, u32[]{:S(2)}, u32[]{:S(2)}) async-start(bf16[128,32,256]{2,0,1:T(8,128)(2,1)} %bitcast.44), calls=%async_computation | async-start | bytes 4194304 | tf_op jit(solution)/shard_map/all_to_all | solution.py:71
  30.6 0.0 all-reduce.3.cloned.1.call-start
  30.7 0.0 copy-done.1
  30.7 0.1 copy.34
  30.8 54.8 %all-to-all-done = bf16[128,32,256]{2,0,1:T(8,128)(2,1)} async-done(((bf16[128,32,256]{2,0,1:T(8,128)(2,1)}), bf16[128,32,256]{2,0,1:T(8,128)(2,1)}, u32[]{:S(2)}, u32[]{:S(2)}) %all-to-all-start) | async-done | bytes 2097184 | tf_op jit(solution)/shard_map/all_to_all | solution.py:71
  85.6 35.3 %all-gather.4.cloned.1.call-done = bf16[4096,512]{0,1:T(8,128)(2,1)} async-done(((bf16[128,512]{0,1:T(8,128)(2,1)}), bf16[4096,512]{0,1:T(8,128)(2,1)}) %all-gather.4.cloned.1.call-update) | async-done | bytes 4194320 | tf_op jit(solution)/shard_map/all_gather | solution.py:87
  120.9 0.0 copy-start.2
  120.9 4.8 multiply_reduce_fusion.1
  125.7 55.3 %psum.28 = f32[]{:T(128)} all-reduce(f32[]{:T(128)} %get-tuple-element.18), channel_id=1, replica_groups=mesh['island'=16,'fsdp'=32] {'fsdp'}, use_global_device_ids=true, to_apply=%region_5.6 | all-reduce | flops 1 | bytes 8 | tf_op jit(solution)/shard_map/psum | solution.py:93
  181.0 0.2 copy.40
  181.9 0.9 convert_subtract_fusion.1
  182.8 0.0 all-reduce.3.cloned.1.call-update
  182.8 0.0 all-reduce.5.cloned.1.call-start
  182.9 16.3 %all-gather.6.cloned.1.call-done = bf16[1,8192,512]{2,1,0:T(8,128)(2,1)} async-done(((bf16[1,256,512]{2,1,0:T(8,128)(2,1)}), bf16[1,8192,512]{2,1,0:T(8,128)(2,1)}) %all-gather.6.cloned.1.call-update) | async-done | bytes 8388624 | tf_op jit(solution)/shard_map/all_gather | solution.py:75
  199.2 0.0 copy-done.2
  199.2 6.6 fusion.1
  205.7 0.0 copy-start.3
  205.8 0.0 copy-start.4
  205.8 0.0 copy-start.5
  205.8 0.0 copy-start.6
  205.8 2.3 fusion.24
  208.1 0.0 all-reduce.5.cloned.1.call-update
  208.1 161.1 %all-reduce.3.cloned.1.call-done = f32[256,512]{0,1:T(8,128)} async-done(((f32[256,512]{0,1:T(8,128)}), f32[256,512]{0,1:T(8,128)}) %all-reduce.3.cloned.1.call-update) | async-done | bytes 524304 | tf_op jit(solution)/shard_map/psum | solution.py:103
  369.2 0.0 copy-done.3
  369.2 0.0 copy-done.4
  369.2 1.4 multiply_subtract_fusion
  370.6 231.6 %all-reduce.5.cloned.1.call-done = f32[16,8192]{1,0:T(8,128)} async-done(((f32[16,8192]{1,0:T(8,128)}), f32[16,8192]{1,0:T(8,128)}) %all-reduce.5.cloned.1.call-update) | async-done | bytes 524304 | tf_op jit(solution)/shard_map/psum | solution.py:83
  602.2 1.8 multiply_reduce_fusion
  604.7 0.7 convert_subtract_fusion.2
  605.4 78.1 %psum.31 = f32[16,256]{1,0:T(8,128)S(1)} all-reduce(f32[16,256]{1,0:T(8,128)S(1)} %convert_subtract_fusion.2), channel_id=1, replica_groups=mesh['island'=16,'fsdp'=32] {'island'}, use_global_device_ids=true, to_apply=%region_9.10 | all-reduce | flops 4096 | bytes 32768 | tf_op jit(solution)/shard_map/psum | solution.py:103
  683.5 0.0 copy-done.5
  683.5 0.0 copy-done.6
  683.5 0.6 multiply_subtract_fusion.2
  (3 shorter events, 0.0 us)
Async XLA Ops:
  7.2 113.7 %all-gather.4.cloned.1.call-start = ((), (), s32[]{:S(2)}) async-start(), calls=%async_computation.1 | async-start | bytes 4325376 | tf_op jit(solution)/shard_map/all_gather | solution.py:87
  13.5 3.6 copy-start
  16.4 1.9 copy-start.7
  16.4 1.9 copy-start.8
  16.4 182.7 %all-gather.6.cloned.1.call-start = ((), (), s32[]{:S(2)}) async-start(), calls=%async_computation.4 | async-start | bytes 8650752 | tf_op jit(solution)/shard_map/all_gather | solution.py:75
  19.1 11.6 %copy-start.1 = (bf16[1,256,512]{2,1,0:T(8,128)(2,1)S(1)}, bf16[1,256,512]{2,1,0:T(8,128)(2,1)}, u32[]{:S(2)}) copy-start(bf16[1,256,512]{2,1,0:T(8,128)(2,1)} %param.16) | copy-start | bytes 786436
  20.7 64.9 %all-to-all-start = ((bf16[128,32,256]{2,0,1:T(8,128)(2,1)}), bf16[128,32,256]{2,0,1:T(8,128)(2,1)}, u32[]{:S(2)}, u32[]{:S(2)}) async-start(bf16[128,32,256]{2,0,1:T(8,128)(2,1)} %bitcast.44), calls=%async_computation | async-start | bytes 4194304 | tf_op jit(solution)/shard_map/all_to_all | solution.py:71
  30.6 338.6 %all-reduce.3.cloned.1.call-start = ((), (), s32[]{:S(2)}) async-start(), calls=%async_computation.2 | async-start | bytes 1048576 | tf_op jit(solution)/shard_map/psum | solution.py:103
  120.9 78.3 %copy-start.2 = (bf16[4,128,128]{1,2,0:T(8,128)(2,1)S(1)}, bf16[4,128,128]{1,2,0:T(8,128)(2,1)}, u32[]{:S(2)}) copy-start(bf16[4,128,128]{1,2,0:T(8,128)(2,1)} %fusion.8) | copy-start | bytes 393220
  182.8 419.4 %all-reduce.5.cloned.1.call-start = ((), (), s32[]{:S(2)}) async-start(), calls=%async_computation.3 | async-start | bytes 1048576 | tf_op jit(solution)/shard_map/psum | solution.py:83
  205.7 163.4 %copy-start.3 = (f32[256,32]{0,1:T(8,128)S(1)}, f32[256,32]{0,1:T(8,128)}, u32[]{:S(2)}) copy-start(f32[256,32]{0,1:T(8,128)} %param.18) | copy-start | bytes 98308
  205.8 163.4 %copy-start.4 = (f32[256,32]{0,1:T(8,128)S(1)}, f32[256,32]{0,1:T(8,128)}, u32[]{:S(2)}) copy-start(f32[256,32]{0,1:T(8,128)} %param.19) | copy-start | bytes 98308
  205.8 477.7 %copy-start.5 = (f32[1,256]{1,0:T(1,128)S(1)}, f32[1,256]{1,0:T(1,128)}, u32[]{:S(2)}) copy-start(f32[1,256]{1,0:T(1,128)} %param.20) | copy-start | bytes 3076
  205.8 477.7 %copy-start.6 = (f32[1,256]{1,0:T(1,128)S(1)}, f32[1,256]{1,0:T(1,128)}, u32[]{:S(2)}) copy-start(f32[1,256]{1,0:T(1,128)} %param.21) | copy-start | bytes 3076
Sparse Core Ops, SparseCore 0:
  16.5 104.2 all-gather.3
  123.0 76.1 all-gather.5
  202.1 167.0 all-reduce.2
  371.9 230.2 all-reduce.4
where the time goes:
time: 691 us
  waiting for transfers between devices  500 us (72%)
  blocking collectives  133 us (19%)
  matrix products  19.6 us (3%)
  between operations  15.3 us (2%)
  starting transfers between devices  10.1 us (1%)
    psum x1, waiting for transfers between devices, body(): gain_grad = lax.psum(gain_part, 'fsdp')  232 us
    psum x1, waiting for transfers between devices, body(): total_wv, total_gain = lax.psum((new_wv, new_gain), 'island')  161 us
    psum x1, blocking collectives, body(): total_wv, total_gain = lax.psum((new_wv, new_gain), 'island')  78.1 us
    psum x1, blocking collectives, body(): weight_square = lax.psum(wv_square, 'fsdp')  55.3 us
    all_to_all x1, waiting for transfers between devices, body(): lax.all_to_all(normed, 'fsdp', split_axis=1, concat_axis=0, tiled=True)  54.8 us
    all_gather x1, waiting for transfers between devices, body(): lax.all_gather(values_grad, 'fsdp', axis=0, tiled=True)  35.3 us
    all_gather x1, waiting for transfers between devices, body(): lax.all_gather(weight_rows, 'fsdp', axis=0, tiled=True)  16.3 us
  transfers between devices with their start and end apart: 5, of which 5 were waited for; matrix products, arithmetic and copies ran while one was open for 3% of the time, Pallas kernels for 0%

commit v1 on v0

--- a/solution.py
+++ b/solution.py
@@ -84,7 +84,10 @@
     wv_grad = (
         jnp.dot(
             col_normed.T,
-            lax.all_gather(values_grad, "fsdp", axis=0, tiled=True),
+            jnp.concatenate(
+                lax.all_to_all(jnp.stack([values_grad] * lax.axis_size("fsdp")), "fsdp", 0, 0),
+                axis=0,
+            ),
             preferred_element_type=jnp.float32,
         )
         * weight_scale

time: 691 us -> 764 us (1.11)
  waiting for transfers between devices: 500 us -> 550 us
  starting transfers between devices: 10.1 us -> 19.9 us
    all_to_all x0 -> x1, waiting for transfers between devices: none -> 101 us  [body(): lax.all_to_all(jnp.stack([values_grad] * lax.axis_size('fsdp')), 'fsdp',...]
    all_gather x1 -> x0, waiting for transfers between devices: 35.3 us -> none  [body(): lax.all_gather(values_grad, 'fsdp', axis=0, tiled=True)]
    all_gather x1, waiting for transfers between devices: 16.3 us -> 0.02 us  [body(): lax.all_gather(weight_rows, 'fsdp', axis=0, tiled=True)]
    all_to_all x0 -> x1, starting transfers between devices: none -> 9.71 us  [body(): lax.all_to_all(jnp.stack([values_grad] * lax.axis_size('fsdp')), 'fsdp',...]
  transfers between devices with their start and end apart: 5 -> 5, of which waited for: 5 -> 4; matrix products, arithmetic and copies ran while one was open for 3% -> 5% of each run, Pallas kernels for 0% -> 0%
where the time goes in v1:
time: 764 us; the launch traced here: 763 us
  waiting for transfers between devices  550 us (72%)
  blocking collectives  133 us (17%)
  matrix products  22 us (3%)
  starting transfers between devices  19.9 us (3%)
  between operations  17.1 us (2%)
  local copies, waits for them, and re-layouts  11 us (1%)
  other arithmetic  9.69 us (1%)
    psum x1, waiting for transfers between devices, body(): gain_grad = lax.psum(gain_part, 'fsdp')  231 us
    psum x1, waiting for transfers between devices, body(): total_wv, total_gain = lax.psum((new_wv, new_gain), 'island')  157 us
    all_to_all x1, waiting for transfers between devices, body(): lax.all_to_all(jnp.stack([values_grad] * lax.axis_size('fsdp')), 'fsdp',...  101 us
    psum x1, blocking collectives, body(): total_wv, total_gain = lax.psum((new_wv, new_gain), 'island')  78.1 us
    all_to_all x1, waiting for transfers between devices, body(): lax.all_to_all(normed, 'fsdp', split_axis=1, concat_axis=0, tiled=True)  59.7 us
    psum x1, blocking collectives, body(): weight_square = lax.psum(wv_square, 'fsdp')  55.4 us
  transfers between devices with their start and end apart: 5, of which 4 were waited for; matrix products, arithmetic and copies ran while one was open for 5% of the time, Pallas kernels for 0%

profile of v1, /device:TPU:32, one launch (start us, length us, event | category | flops | bytes accessed | tf_op | source)
XLA Modules:
  0.0 762.8 jit_solution(4802255863670906482)
XLA Ops:
  8.0 0.0 copy-start
  8.0 0.0 copy-start.8
  8.0 0.0 copy-start.9
  8.0 0.0 all-gather.3.cloned.1.call-start
  8.1 0.7 all-gather.3.cloned.1.call-update
  8.8 1.9 convert_reduce_fusion
  10.7 2.3 fusion.6
  13.0 0.0 copy-done
  13.0 0.0 copy-done.8
  13.1 0.0 copy-done.9
  13.1 2.1 fusion.2
  15.2 0.0 copy-start.1
  15.2 4.2 copy.37
  19.3 0.0 copy-start.3
  19.3 10.0 %all-to-all-start = ((bf16[128,32,256]{0,2,1:T(8,128)(2,1)}), bf16[128,32,256]{0,2,1:T(8,128)(2,1)}, u32[]{:S(2)}, u32[]{:S(2)}) async-start(bf16[128,32,256]{0,2,1:T(8,128)(2,1)} %bitcast.46), calls=%async_computation | async-start | bytes 4194304 | tf_op jit(solution)/shard_map/all_to_all | solution.py:71
  29.4 0.0 copy-done.1
  29.4 1.3 copy.41
  30.6 0.0 copy-done.3
  30.7 1.6 copy.40
  32.3 3.5 fusion.38
  35.8 2.1 fusion.13
  37.9 0.1 copy.32
  38.0 59.7 %all-to-all-done = bf16[128,32,256]{0,2,1:T(8,128)(2,1)} async-done(((bf16[128,32,256]{0,2,1:T(8,128)(2,1)}), bf16[128,32,256]{0,2,1:T(8,128)(2,1)}, u32[]{:S(2)}, u32[]{:S(2)}) %all-to-all-start) | async-done | bytes 2097184 | tf_op jit(solution)/shard_map/all_to_all | solution.py:71
  97.7 2.4 stack.2
  100.2 0.0 copy-start.2
  100.2 9.7 %all-to-all-start.1 = ((bf16[32,128,512]{2,1,0:T(8,128)(2,1)}), bf16[32,128,512]{2,1,0:T(8,128)(2,1)}, u32[]{:S(2)}, u32[]{:S(2)}) async-start(bf16[32,128,512]{2,1,0:T(8,128)(2,1)} %stack.2), calls=%async_computation.1 | async-start | bytes 8388608 | tf_op jit(solution)/shard_map/all_to_all | solution.py:88
  109.9 0.0 all-reduce.3.cloned.1.call-start
  109.9 0.0 copy-done.2
  109.9 0.1 copy.26
  110.1 101.1 %all-to-all-done.1 = bf16[32,128,512]{2,1,0:T(8,128)(2,1)} async-done(((bf16[32,128,512]{2,1,0:T(8,128)(2,1)}), bf16[32,128,512]{2,1,0:T(8,128)(2,1)}, u32[]{:S(2)}, u32[]{:S(2)}) %all-to-all-start.1) | async-done | bytes 4194336 | tf_op jit(solution)/shard_map/all_to_all | solution.py:88
  211.1 5.5 multiply_reduce_fusion.1
  216.6 55.4 %psum.28 = f32[]{:T(128)} all-reduce(f32[]{:T(128)} %get-tuple-element.14), channel_id=1, replica_groups=mesh['island'=16,'fsdp'=32] {'fsdp'}, use_global_device_ids=true, to_apply=%region_5.6 | all-reduce | flops 1 | bytes 8 | tf_op jit(solution)/shard_map/psum | solution.py:96
  272.0 1.2 copy.33
  274.0 0.9 convert_subtract_fusion.1
  274.9 0.0 all-reduce.3.cloned.1.call-update
  274.9 0.0 all-reduce.5.cloned.1.call-start
  275.0 0.0 all-gather.3.cloned.1.call-done
  275.0 6.6 fusion.1
  281.6 0.0 copy-start.4
  281.6 0.0 copy-start.5
  281.6 0.0 copy-start.6
  281.6 0.0 copy-start.7
  281.6 2.3 fusion.29
  283.9 0.0 all-reduce.5.cloned.1.call-update
  283.9 156.8 %all-reduce.3.cloned.1.call-done = f32[256,512]{0,1:T(8,128)} async-done(((f32[256,512]{0,1:T(8,128)}), f32[256,512]{0,1:T(8,128)}) %all-reduce.3.cloned.1.call-update) | async-done | bytes 524304 | tf_op jit(solution)/shard_map/psum | solution.py:106
  440.7 0.0 copy-done.4
  440.7 0.0 copy-done.5
  440.7 1.4 multiply_subtract_fusion
  442.1 231.4 %all-reduce.5.cloned.1.call-done = f32[16,8192]{1,0:T(8,128)} async-done(((f32[16,8192]{1,0:T(8,128)}), f32[16,8192]{1,0:T(8,128)}) %all-reduce.5.cloned.1.call-update) | async-done | bytes 524304 | tf_op jit(solution)/shard_map/psum | solution.py:83
  673.5 1.8 multiply_reduce_fusion
  676.0 0.7 convert_subtract_fusion.2
  676.7 78.1 %psum.31 = f32[16,256]{1,0:T(8,128)S(1)} all-reduce(f32[16,256]{1,0:T(8,128)S(1)} %convert_subtract_fusion.2), channel_id=1, replica_groups=mesh['island'=16,'fsdp'=32] {'island'}, use_global_device_ids=true, to_apply=%region_9.10 | all-reduce | flops 4096 | bytes 32768 | tf_op jit(solution)/shard_map/psum | solution.py:106
  754.8 0.0 copy-done.6
  754.8 0.0 copy-done.7
  754.8 0.6 multiply_subtract_fusion.2
  (4 shorter events, 0.1 us)
Async XLA Ops:
  8.0 5.0 copy-start
  8.0 5.0 copy-start.8
  8.0 5.0 copy-start.9
  8.0 267.0 %all-gather.3.cloned.1.call-start = ((), (), s32[]{:S(2)}) async-start(), calls=%async_computation.4 | async-start | bytes 8650752 | tf_op jit(solution)/shard_map/all_gather | solution.py:75
  15.2 14.2 %copy-start.1 = (bf16[128,4096]{1,0:T(8,128)(2,1)S(1)}, bf16[128,4096]{1,0:T(8,128)(2,1)}, u32[]{:S(2)}) copy-start(bf16[128,4096]{1,0:T(8,128)(2,1)} %param.13) | copy-start | bytes 3145732
  19.3 11.3 %copy-start.3 = (bf16[128,512]{1,0:T(8,128)(2,1)S(1)}, bf16[128,512]{1,0:T(8,128)(2,1)}, u32[]{:S(2)}) copy-start(bf16[128,512]{1,0:T(8,128)(2,1)} %param.14) | copy-start | bytes 393220
  19.3 78.4 %all-to-all-start = ((bf16[128,32,256]{0,2,1:T(8,128)(2,1)}), bf16[128,32,256]{0,2,1:T(8,128)(2,1)}, u32[]{:S(2)}, u32[]{:S(2)}) async-start(bf16[128,32,256]{0,2,1:T(8,128)(2,1)} %bitcast.46), calls=%async_computation | async-start | bytes 4194304 | tf_op jit(solution)/shard_map/all_to_all | solution.py:71
  100.2 9.8 %copy-start.2 = (bf16[1,256,512]{2,1,0:T(8,128)(2,1)S(1)}, bf16[1,256,512]{2,1,0:T(8,128)(2,1)}, u32[]{:S(2)}) copy-start(bf16[1,256,512]{2,1,0:T(8,128)(2,1)} %param.16) | copy-start | bytes 786436
  100.2 111.0 %all-to-all-start.1 = ((bf16[32,128,512]{2,1,0:T(8,128)(2,1)}), bf16[32,128,512]{2,1,0:T(8,128)(2,1)}, u32[]{:S(2)}, u32[]{:S(2)}) async-start(bf16[32,128,512]{2,1,0:T(8,128)(2,1)} %stack.2), calls=%async_computation.1 | async-start | bytes 8388608 | tf_op jit(solution)/shard_map/all_to_all | solution.py:88
  109.9 330.8 %all-reduce.3.cloned.1.call-start = ((), (), s32[]{:S(2)}) async-start(), calls=%async_computation.2 | async-start | bytes 1048576 | tf_op jit(solution)/shard_map/psum | solution.py:106
  274.9 398.6 %all-reduce.5.cloned.1.call-start = ((), (), s32[]{:S(2)}) async-start(), calls=%async_computation.3 | async-start | bytes 1048576 | tf_op jit(solution)/shard_map/psum | solution.py:83
  281.6 159.1 %copy-start.4 = (f32[256,32]{0,1:T(8,128)S(1)}, f32[256,32]{0,1:T(8,128)}, u32[]{:S(2)}) copy-start(f32[256,32]{0,1:T(8,128)} %param.18) | copy-start | bytes 98308
  281.6 159.1 %copy-start.5 = (f32[256,32]{0,1:T(8,128)S(1)}, f32[256,32]{0,1:T(8,128)}, u32[]{:S(2)}) copy-start(f32[256,32]{0,1:T(8,128)} %param.19) | copy-start | bytes 98308
  281.6 473.2 %copy-start.6 = (f32[1,256]{1,0:T(1,128)S(1)}, f32[1,256]{1,0:T(1,128)}, u32[]{:S(2)}) copy-start(f32[1,256]{1,0:T(1,128)} %param.20) | copy-start | bytes 3076
  281.6 473.2 %copy-start.7 = (f32[1,256]{1,0:T(1,128)S(1)}, f32[1,256]{1,0:T(1,128)}, u32[]{:S(2)}) copy-start(f32[1,256]{1,0:T(1,128)} %param.21) | copy-start | bytes 3076
Sparse Core Ops, SparseCore 0:
  11.0 138.4 all-gather.2
Sparse Core Ops, SparseCore 1:
  275.0 165.6 all-reduce.2
  443.5 230.0 all-reduce.4
